TPU v7x, 256 devices: a whole 4x4x8 slice. The times are simulated.
256 devices in a mesh: dp: 16 (over y, x), section: 2 (over core), tensor: 8 (over z).
Axes of the slice: x: 4, y: 4, z: 8, core: 2. Of those that a mesh axis runs over, the one named last changes fastest.
Arguments:
- tokens: bfloat16 [2048, 16384], P('dp'), may hold values from -9 to 9
- order: int32 [2048], replicated, may hold values from 0 to 2047, as said below
- segments: int32 [2048], replicated, may hold values from 0 to 1, as said below
- gain: float32 [2, 16384], P('section', 'dp'), may hold values from 0.1 to 1.9
- w_query: bfloat16 [2, 16384, 8192], P('section', 'dp', 'tensor'), may hold values from -0.046875 to 0.046875
- key_value_weight: bfloat16 [2, 16384, 8, 256], P('section', 'dp', 'tensor'), may hold values from -0.046875 to 0.046875
- w_out: bfloat16 [2, 8192, 16384], P('section', 'tensor', 'dp'), may hold values from -0.0625 to 0.0625
Outputs:
- layer_out: bfloat16 [2048, 16384], P('section', 'dp')
Inputs may be any that keep to these rules, and one draw needn't show every extreme that they name: A permutation that moves whole sentences: the rows of one sentence (a run of equal segments within a block of 32 rows) come from consecutive entry rows in order. `segments`: within each block of 32 rows the sentence numbers do not fall and each of 0 to 1 appears.
All inputs are finite; a program needn't handle non-finite values.
Results may differ from a plain program's by a relative error of at most 0.022.
Values may be sent and summed in bfloat16 or wider, within the bound.
No kernel may reach another device: no remote copies, remote signals or barrier semaphores. Data moves between devices by JAX's collectives and lax.ppermute only.
A program may use at most 64 MiB of HBM per device.

v0:
```python
import math
import jax
import jax.numpy as jnp
from jax import lax
from jax.experimental.layout import Layout, with_layout_constraint
from jax.sharding import PartitionSpec as P

MODEL_WIDTH = 16384
KEYVALUE_HEADS = 8
QUERY_HEADS = 64
MICRO_TOKENS = 32
HEAD_WIDTH = 128
SPARE_COLUMNS = 128
M = 4
norm_epsilon = 1e-05


def causal_block_attend(query_rows, key_value_rows, allowed, query_group_width):
    block_count, row_count = allowed.shape[:2]
    kv_heads = key_value_rows.shape[1]
    head_size = key_value_rows.shape[2] // 2
    query_head_rows = query_rows.reshape(
        block_count, row_count, kv_heads, query_group_width, head_size
    )
    key_value_blocks = key_value_rows.reshape(block_count, row_count, kv_heads, 2 * head_size)
    key_heads = key_value_blocks[..., :head_size]
    value_heads = key_value_blocks[..., head_size:]
    scores = jnp.einsum(
        "bqkgd,bskd->bkgqs", query_head_rows, key_heads, preferred_element_type=jnp.float32
    ) / math.sqrt(head_size)
    raw_weights = jnp.where(allowed[:, None, None], jnp.exp(scores), 0.0)
    totals = jnp.sum(raw_weights, axis=-1, keepdims=True)
    probs = (raw_weights / totals).astype(jnp.bfloat16)
    attended_rows = jnp.einsum(
        "bkgqs,bskd->bqkgd", probs, value_heads, preferred_element_type=jnp.float32
    )
    return attended_rows.astype(jnp.bfloat16).reshape(
        block_count * row_count, kv_heads * query_group_width * head_size
    )


def block_mask(sentence_segment_rows):
    row_count = sentence_segment_rows.shape[1]
    position = jnp.arange(row_count)
    return (sentence_segment_rows[:, :, None] == sentence_segment_rows[:, None, :]) & (
        position[None, :] <= position[:, None]
    )[None]


def gathered_over(block, axis):
    count = lax.axis_size(axis)
    spread = jnp.broadcast_to(block[None], (count,) + block.shape)
    return lax.all_to_all(spread, axis, 0, 0, tiled=False).reshape(
        (count * block.shape[0],) + block.shape[1:]
    )


def section_layer(hidden, own_allowed, gain_row, joined_weight, out_weight):
    row_count = hidden.shape[0]
    group_count = lax.axis_size("dp")
    own_rows = row_count // group_count
    widened = hidden.astype(jnp.float32)
    normed_rows = (widened * gain_row[None, :]).astype(jnp.bfloat16)
    joined_terms = jnp.dot(normed_rows, joined_weight, preferred_element_type=jnp.float32)
    query_width = out_weight.shape[0]
    keyval_width = joined_terms.shape[1] - query_width - SPARE_COLUMNS
    square_terms = jnp.sum(widened * widened, axis=1, keepdims=True)
    square_high = lax.reduce_precision(square_terms, exponent_bits=8, mantissa_bits=7)
    square_low = square_terms - square_high
    column = lax.broadcasted_iota(jnp.int32, joined_terms.shape, 1)
    square_column = query_width + keyval_width
    payload = jnp.where(
        column == square_column,
        square_high,
        jnp.where(column == square_column + 1, square_low, joined_terms),
    ).astype(jnp.bfloat16)
    arrived = lax.all_to_all(
        payload.reshape(group_count, own_rows, payload.shape[1]), "dp", 0, 0, tiled=False
    )
    summed = jnp.sum(arrived.astype(jnp.float32), axis=0)
    own_squares = summed[:, query_width + keyval_width] + summed[:, query_width + keyval_width + 1]
    root_mean_square = jnp.sqrt(own_squares / MODEL_WIDTH + norm_epsilon)
    scaled_sums = summed[:, : query_width + keyval_width] / root_mean_square[:, None]
    query_rows = scaled_sums[:, :query_width].astype(jnp.bfloat16)
    key_value_rows = (
        scaled_sums[:, query_width:].astype(jnp.bfloat16).reshape(own_rows, -1, 2 * HEAD_WIDTH)
    )
    attended_rows = causal_block_attend(
        query_rows, key_value_rows, own_allowed, QUERY_HEADS // KEYVALUE_HEADS
    )
    head_terms = jnp.dot(
        gathered_over(attended_rows, "dp"), out_weight, preferred_element_type=jnp.float32
    )
    head_total = lax.psum(head_terms.astype(jnp.bfloat16), "tensor").astype(jnp.float32)
    return (widened + head_total).astype(jnp.bfloat16)


def on_device(tokens, order, segments, gain, w_query, key_value_weight, w_out):
    section_count = lax.axis_size("section")
    section_index = lax.axis_index("section")
    group_count = lax.axis_size("dp")
    slice_width = w_query.shape[1]
    joined = jnp.concatenate(
        [
            w_query[0],
            key_value_weight[0].reshape(slice_width, -1),
            jnp.zeros((slice_width, SPARE_COLUMNS), w_query.dtype),
        ],
        axis=1,
    )
    own = (gain[0], joined, w_out[0])
    swap = [(i, (i + 1) % section_count) for i in range(section_count)]
    other = lax.ppermute(own, "section", swap)
    entry_rows, model_width = tokens.shape
    part_rows = entry_rows // section_count
    my_rows = lax.dynamic_slice_in_dim(tokens, section_index * part_rows, part_rows)
    got = lax.all_to_all(
        my_rows.reshape(part_rows, group_count, model_width // group_count), "dp", 1, 0, tiled=True
    ).reshape(group_count * part_rows, -1)
    received = lax.ppermute(got, "section", swap)
    rows_here = group_count * entry_rows // section_count
    own_blocks = rows_here // (group_count * MICRO_TOKENS)
    own_segments = lax.dynamic_slice_in_dim(
        segments,
        section_index * rows_here + lax.axis_index("dp") * own_blocks * MICRO_TOKENS,
        own_blocks * MICRO_TOKENS,
    ).reshape(own_blocks, MICRO_TOKENS)
    other, received, own_allowed = lax.optimization_barrier(
        (other, received, block_mask(own_segments))
    )
    my_order = lax.dynamic_slice_in_dim(order, section_index * rows_here, rows_here)
    source_group = my_order // entry_rows
    within = my_order % entry_rows
    from_other = within // part_rows != section_index
    block_index = source_group * part_rows + within % part_rows
    hits = lax.broadcasted_iota(jnp.int32, (rows_here, got.shape[0]), 1) == block_index[:, None]
    picked_here = (hits & ~from_other[:, None]).astype(got.dtype)
    picked_there = (hits & from_other[:, None]).astype(got.dtype)
    hidden = (
        jnp.dot(picked_here, got, preferred_element_type=jnp.float32)
        + jnp.dot(picked_there, received, preferred_element_type=jnp.float32)
    ).astype(got.dtype)
    hidden = with_layout_constraint(hidden, Layout(major_to_minor=(0, 1)))
    for layer_index in range(section_count):
        params = jax.tree.map(
            lambda mine, theirs: jnp.where(section_index == layer_index, mine, theirs), own, other
        )
        hidden = section_layer(hidden, own_allowed, *params)
    return hidden


def solution(mesh):
    placed = (
        P("dp", None),
        P(),
        P(),
        P("section", "dp"),
        P("section", "dp", "tensor"),
        P("section", "dp", "tensor", None),
        P("section", "tensor", "dp"),
    )
    return jax.shard_map(
        on_device, mesh=mesh, in_specs=placed, out_specs=P("section", "dp"), check_vma=False
    )
```

profile of v0, /device:TPU:2, one launch (start us, length us, event | category | flops | bytes accessed | tf_op | source)
XLA Modules:
  0.0 392.8 jit_solution(6139880613853147727)
XLA Ops:
  6.5 1.7 constant_dynamic-slice_fusion
  8.3 1.6 copy.54
  9.8 7.7 %all-to-all-start = ((bf16[64,16,1024]{2,0,1:T(8,128)(2,1)}), bf16[64,16,1024]{2,0,1:T(8,128)(2,1)}, u32[]{:S(2)}, u32[]{:S(2)}) async-start(bf16[64,16,1024]{2,0,1:T(8,128)(2,1)} %bitcast.102), calls=%async_computation | async-start | bytes 4194304 | tf_op jit(solution)/shard_map/all_to_all | solution.py:117
  17.7 2.2 maximum_maximum_fusion
  19.9 0.5 collective-permute-start.2
  20.4 24.4 %all-to-all-done = bf16[64,16,1024]{2,0,1:T(8,128)(2,1)} async-done(((bf16[64,16,1024]{2,0,1:T(8,128)(2,1)}), bf16[64,16,1024]{2,0,1:T(8,128)(2,1)}, u32[]{:S(2)}, u32[]{:S(2)}) %all-to-all-start) | async-done | bytes 2097184 | tf_op jit(solution)/shard_map/all_to_all | solution.py:117
  44.8 0.5 collective-permute-start
  45.3 0.8 dynamic_slice.11
  46.3 4.0 %fusion.8 = f32[1024,1024]{1,0:T(8,128)S(1)} fusion(bf16[1024,1024]{1,0:T(8,128)(2,1)} %bitcast.2, s32[1024]{0:T(1024)S(1)} %fusion.61, pred[1024]{0:T(1024)(128)(4,1)S(1)} %get-tuple-element.15), kind=kOutput, calls=%fused_computation.20 | convolution fusion | flops 2149580800 | bytes 6296576 | tf_op jit(solution)/shard_map/dot_general | solution.py:140
  50.4 4.9 %fusion = (f32[1024]{0:T(1024)S(1)}, bf16[1024,1024]{1,0:T(8,128)(2,1)S(1)}) fusion(f32[1024,1024]{1,0:T(8,128)S(1)} %fusion.8, bf16[1024,1024]{1,0:T(8,128)(2,1)} %collective-permute-done.3, s32[1024]{0:T(1024)S(1)} %fusion.61, pred[1024]{0:T(1024)(128)(4,1)S(1)} %get-tuple-element.16), kind=kOutput, calls=%fused_computation.10 | convolution fusion | flops 2154822656 | bytes 8397824 | tf_op jit(solution)/shard_map/dot_general | solution.py:141
  55.3 3.6 select_convert_fusion.1
  58.9 44.4 %all_to_all.35 = bf16[16,64,1408]{2,1,0:T(8,128)(2,1)S(1)} all-to-all(bf16[16,64,1408]{2,1,0:T(8,128)(2,1)S(1)} %bitcast.107), channel_id=1, replica_groups=mesh['dp'=16,'section'=2,'tensor'=8] {'dp'}, dimensions={0} | all-to-all | bytes 5767168 | tf_op jit(solution)/shard_map/all_to_all | solution.py:77
  103.3 0.4 convert_reduce_fusion.1
  104.9 32.2 %all_to_all.36 = bf16[16,64,1024]{2,1,0:T(8,128)(2,1)S(1)} all-to-all(bf16[16,64,1024]{2,1,0:T(8,128)(2,1)S(1)} %broadcast_in_dim.78), channel_id=1, replica_groups=mesh['dp'=16,'section'=2,'tensor'=8] {'dp'}, dimensions={0} | all-to-all | bytes 4194304 | tf_op jit(solution)/shard_map/all_to_all | solution.py:53
  137.1 5.3 %fusion.30 = bf16[1024,1024]{1,0:T(8,128)(2,1)} fusion(bf16[1024,1024]{1,0:T(8,128)(2,1)S(1)} %bitcast.112, bf16[1024,1024]{1,0:T(8,128)(2,1)} %collective-permute-done.2, pred[]{:T(512)S(6)} %eq.58, bf16[1,1024,1024]{2,1,0:T(8,128)(2,1)} %param.13), kind=kOutput, calls=%fused_computation.40 | convolution fusion | flops 2149580800 | bytes 8388609 | tf_op jit(solution)/shard_map/dot_general | solution.py:91
  142.4 82.2 %all-reduce.3.cloned.1.call-done = bf16[1024,1024]{1,0:T(8,128)(2,1)} async-done(((bf16[1024,1024]{1,0:T(8,128)(2,1)}), bf16[1024,1024]{1,0:T(8,128)(2,1)}) %all-reduce.3.cloned.1.call-update) | async-done | bytes 2097168 | tf_op jit(solution)/shard_map/psum | solution.py:94
  224.6 2.5 fusion.3
  227.5 5.4 %select_convert_fusion = bf16[1024,1408]{1,0:T(8,128)(2,1)S(1)} fusion(bf16[1024,1408]{1,0:T(8,128)(2,1)} %collective-permute-done.1, bf16[1024]{0:T(1024)(128)(2,1)S(1)} %get-tuple-element.20, bf16[1024]{0:T(1024)(128)(2,1)S(1)} %get-tuple-element.19, pred[]{:T(512)S(6)} %eq.59, pred[1408]{0:T(1024)(128)(4,1)S(1)} %get-tuple-element.29, ...), kind=kOutput, calls=%fused_computation.7 | convolution fusion | flops 2973106176 | bytes 12596737 | tf_op jit(solution)/shard_map/dot_general | solution.py:64
  232.9 37.0 %all_to_all.37 = bf16[16,64,1408]{2,1,0:T(8,128)(2,1)S(1)} all-to-all(bf16[16,64,1408]{2,1,0:T(8,128)(2,1)S(1)} %bitcast.106), channel_id=1, replica_groups=mesh['dp'=16,'section'=2,'tensor'=8] {'dp'}, dimensions={0} | all-to-all | bytes 5767168 | tf_op jit(solution)/shard_map/all_to_all | solution.py:77
  269.8 0.4 convert_reduce_fusion
  271.5 25.5 %all_to_all.38 = bf16[16,64,1024]{2,1,0:T(8,128)(2,1)S(1)} all-to-all(bf16[16,64,1024]{2,1,0:T(8,128)(2,1)S(1)} %broadcast_in_dim.82), channel_id=1, replica_groups=mesh['dp'=16,'section'=2,'tensor'=8] {'dp'}, dimensions={0} | all-to-all | bytes 4194304 | tf_op jit(solution)/shard_map/all_to_all | solution.py:53
  297.0 5.9 %fusion.33 = bf16[1024,1024]{1,0:T(8,128)(2,1)} fusion(bf16[1024,1024]{1,0:T(8,128)(2,1)S(1)} %bitcast.111, bf16[1024,1024]{1,0:T(8,128)(2,1)} %collective-permute-done.2, pred[]{:T(512)S(6)} %eq.59, bf16[1,1024,1024]{2,1,0:T(8,128)(2,1)} %param.13), kind=kOutput, calls=%fused_computation.41 | convolution fusion | flops 2149580800 | bytes 8388609 | tf_op jit(solution)/shard_map/dot_general | solution.py:91
  302.9 78.0 %all-reduce.5.cloned.1.call-done = bf16[1024,1024]{1,0:T(8,128)(2,1)} async-done(((bf16[1024,1024]{1,0:T(8,128)(2,1)}), bf16[1024,1024]{1,0:T(8,128)(2,1)}) %all-reduce.5.cloned.1.call-update) | async-done | bytes 2097168 | tf_op jit(solution)/shard_map/psum | solution.py:94
  380.9 5.0 %fusion.5 = bf16[1024,1024]{1,0:T(8,128)(2,1)} fusion(bf16[1024,1024]{1,0:T(8,128)(2,1)} %all-reduce.5.cloned.1.call-done, bf16[1024,1024]{1,0:T(8,128)(2,1)} %all-reduce.3.cloned.1.call-done, bf16[1024,1024]{1,0:T(8,128)(2,1)S(1)} %get-tuple-element.24), kind=kLoop, calls=%fused_computation.15 | loop fusion | flops 8388608 | bytes 8388608 | tf_op jit(solution)/shard_map/convert_element_type | solution.py:95
  (55 shorter events, 3.2 us)
Async XLA Ops:
  9.8 7.8 %copy-start.1 = (bf16[1,1024,1024]{2,1,0:T(8,128)(2,1)S(1)}, bf16[1,1024,1024]{2,1,0:T(8,128)(2,1)}, u32[]{:S(2)}) copy-start(bf16[1,1024,1024]{2,1,0:T(8,128)(2,1)} %param.11) | copy-start | bytes 6291460
  9.8 7.8 %copy-start.4 = (bf16[1,1024,1,256]{3,1,2,0:T(8,128)(2,1)S(1)}, bf16[1,1024,1,256]{3,1,2,0:T(8,128)(2,1)}, u32[]{:S(2)}) copy-start(bf16[1,1024,1,256]{3,1,2,0:T(8,128)(2,1)} %param.12) | copy-start | bytes 1572868
  9.8 35.0 %all-to-all-start = ((bf16[64,16,1024]{2,0,1:T(8,128)(2,1)}), bf16[64,16,1024]{2,0,1:T(8,128)(2,1)}, u32[]{:S(2)}, u32[]{:S(2)}) async-start(bf16[64,16,1024]{2,0,1:T(8,128)(2,1)} %bitcast.102), calls=%async_computation | async-start | bytes 4194304 | tf_op jit(solution)/shard_map/all_to_all | solution.py:117
  17.6 27.2 %copy-start.6 = (f32[1,1024]{1,0:T(1,128)S(1)}, f32[1,1024]{1,0:T(1,128)}, u32[]{:S(2)}) copy-start(f32[1,1024]{1,0:T(1,128)} %param.10) | copy-start | bytes 12292
  17.6 28.6 %copy-start.5 = (s32[2048]{0:T(1024)S(1)}, s32[2048]{0:T(1024)}, u32[]{:S(2)}) copy-start(s32[2048]{0:T(1024)} %param.8) | copy-start | bytes 24580
  17.6 207.0 %all-reduce.3.cloned.1.call-start = ((), (), s32[]{:S(2)}) async-start(), calls=%async_computation.5 | async-start | bytes 4194304 | tf_op jit(solution)/shard_map/psum | solution.py:94
  19.9 30.4 %collective-permute-start.1 = (bf16[1024,1408]{1,0:T(8,128)(2,1)}, bf16[1024,1408]{1,0:T(8,128)(2,1)}, u32[]{:S(2)}, u32[]{:S(2)}) collective-permute-start(bf16[1024,1408]{1,0:T(8,128)(2,1)} %maximum_maximum_fusion), channel_id=1, source_target_pairs={{0,8},{8,0},{1,9},{9,1},{2,10},{10,2},{3,11},{11,3},{4,12},{12,4},... | collective-permute-start | bytes 8650760 | tf_op jit(solution)/shard_map/ppermute | solution.py:113
  19.9 30.4 %collective-permute-start.2 = (bf16[1024,1024]{1,0:T(8,128)(2,1)}, bf16[1024,1024]{1,0:T(8,128)(2,1)}, u32[]{:S(2)}, u32[]{:S(2)}) collective-permute-start(bf16[1024,1024]{1,0:T(8,128)(2,1)} %bitcast.6), channel_id=1, source_target_pairs={{0,8},{8,0},{1,9},{9,1},{2,10},{10,2},{3,11},{11,3},{4,12},{12,4},... | collective-permute-start | bytes 6291464 | tf_op jit(solution)/shard_map/ppermute | solution.py:113
  44.8 5.5 %collective-permute-start.3 = (bf16[1024,1024]{1,0:T(8,128)(2,1)}, bf16[1024,1024]{1,0:T(8,128)(2,1)}, u32[]{:S(2)}, u32[]{:S(2)}) collective-permute-start(bf16[1024,1024]{1,0:T(8,128)(2,1)} %bitcast.2), channel_id=1, source_target_pairs={{0,8},{8,0},{1,9},{9,1},{2,10},{10,2},{3,11},{11,3},{4,12},{12,4},... | collective-permute-start | bytes 6291464 | tf_op jit(solution)/shard_map/ppermute | solution.py:120
  44.8 5.5 %collective-permute-start = (f32[1024]{0:T(1024)S(1)}, f32[1024]{0:T(1024)S(1)}, u32[]{:S(2)}, u32[]{:S(2)}) collective-permute-start(f32[1024]{0:T(1024)S(1)} %bitcast.126), channel_id=1, source_target_pairs={{0,8},{8,0},{1,9},{9,1},{2,10},{10,2},{3,11},{11,3},{4,12},{12,4},... | collective-permute-start | bytes 12296 | tf_op jit(solution)/shard_map/ppermute | solution.py:113
  50.3 4.9 %copy-start.2 = (bf16[1,1024,1024]{2,1,0:T(8,128)(2,1)S(1)}, bf16[1,1024,1024]{2,1,0:T(8,128)(2,1)}, u32[]{:S(2)}) copy-start(bf16[1,1024,1024]{2,1,0:T(8,128)(2,1)} %param.11) | copy-start | bytes 6291460
  142.4 238.5 %all-reduce.5.cloned.1.call-start = ((), (), s32[]{:S(2)}) async-start(), calls=%async_computation.6 | async-start | bytes 4194304 | tf_op jit(solution)/shard_map/psum | solution.py:94
  224.6 2.5 copy-start
  224.6 2.9 copy-start.3
Sparse Core Ops, SparseCore 0:
  142.5 82.0 all-reduce.2
  303.1 77.8 all-reduce.4
where the time goes:
time: 393 us
  waiting for transfers between devices  185 us (47%)
  blocking collectives  139 us (35%)
  matrix products  30.1 us (8%)
  between operations  13.7 us (3%)
  other arithmetic  11.2 us (3%)
  starting transfers between devices  8.84 us (2%)
  local copies, waits for them, and re-layouts  5.23 us (1%)
    psum x2, waiting for transfers between devices, section_layer(): lax.psum(head_terms.astype(jnp.bfloat16), 'tensor').astype(jnp.float32)  160 us
    all_to_all x2, blocking collectives, section_layer(): lax.all_to_all(payload.reshape(group_count, own_rows, payload.shape[1]),...  81.4 us
    all_to_all x2, blocking collectives, gathered_over(): lax.all_to_all(spread, axis, 0, 0, tiled=False)  57.7 us
    all_to_all x1, waiting for transfers between devices, on_device(): lax.all_to_all(my_rows.reshape(part_rows, group_count, model_width // gro...  24.4 us
    dot_general x2, matrix products, section_layer(): jnp.dot(gathered_over(attended_rows, 'dp'), out_weight, preferred_element...  11.2 us
    dot_general x2, matrix products, section_layer(): jnp.dot(normed_rows, joined_weight, preferred_element_type=jnp.float32)  8.97 us
  transfers between devices with their start and end apart: 7, of which 3 were waited for; matrix products, arithmetic and copies ran while one was open for 2% of the time, Pallas kernels for 0%

commit v1 on v0

--- a/solution.py
+++ b/solution.py
@@ -114,8 +114,20 @@
     entry_rows, model_width = tokens.shape
     part_rows = entry_rows // section_count
     my_rows = lax.dynamic_slice_in_dim(tokens, section_index * part_rows, part_rows)
-    got = lax.all_to_all(
-        my_rows.reshape(part_rows, group_count, model_width // group_count), "dp", 1, 0, tiled=True
+    got = jnp.concatenate(
+        lax.all_to_all(
+            jnp.stack(
+                jnp.split(
+                    my_rows.reshape(part_rows, group_count, model_width // group_count),
+                    lax.axis_size("dp"),
+                    axis=1,
+                )
+            ),
+            "dp",
+            0,
+            0,
+        ),
+        axis=0,
     ).reshape(group_count * part_rows, -1)
     received = lax.ppermute(got, "section", swap)
     rows_here = group_count * entry_rows // section_count

time: 393 us -> 408 us (1.038)
  local copies, waits for them, and re-layouts: 5.23 us -> 20.6 us
    unnamed x20 -> x34, local copies, waits for them, and re-layouts: 0.47 us -> 12.2 us
    split x0 -> x1, local copies, waits for them, and re-layouts: none -> 4.5 us  [on_device(): jnp.split(my_rows.reshape(part_rows, group_count, model_width // group_co...]
where the time goes in v1:
time: 408 us
  waiting for transfers between devices  184 us (45%)
  blocking collectives  139 us (34%)
  matrix products  30.1 us (7%)
  local copies, waits for them, and re-layouts  20.6 us (5%)
  between operations  13.8 us (3%)
  other arithmetic  11.2 us (3%)
  starting transfers between devices  9.01 us (2%)
    psum x2, waiting for transfers between devices, section_layer(): lax.psum(head_terms.astype(jnp.bfloat16), 'tensor').astype(jnp.float32)  160 us
    all_to_all x2, blocking collectives, section_layer(): lax.all_to_all(payload.reshape(group_count, own_rows, payload.shape[1]),...  81.3 us
    all_to_all x2, blocking collectives, gathered_over(): lax.all_to_all(spread, axis, 0, 0, tiled=False)  57.5 us
    all_to_all x1, waiting for transfers between devices, on_device(): lax.all_to_all(jnp.stack(jnp.split(my_rows.reshape(part_rows, group_count...  24.3 us
    unnamed x34, local copies, waits for them, and re-layouts  12.2 us
    dot_general x2, matrix products, section_layer(): jnp.dot(gathered_over(attended_rows, 'dp'), out_weight, preferred_element...  11.2 us
    dot_general x2, matrix products, section_layer(): jnp.dot(normed_rows, joined_weight, preferred_element_type=jnp.float32)  8.97 us
  transfers between devices with their start and end apart: 7, of which 3 were waited for; matrix products, arithmetic and copies ran while one was open for 2% of the time, Pallas kernels for 0%

profile of v1, /device:TPU:2, one launch (start us, length us, event | category | flops | bytes accessed | tf_op | source)
XLA Modules:
  0.0 407.7 jit_solution(14749154020659762271)
XLA Ops:
  6.5 1.7 constant_dynamic-slice_fusion
  8.3 1.2 copy.236
  9.5 4.5 %fusion.71 = (bf16[64,1,1024]{2,1,0:T(2,128)(2,1)S(1)}, bf16[64,1,1024]{2,1,0:T(2,128)(2,1)S(1)}, bf16[64,1,1024]{2,1,0:T(2,128)(2,1)S(1)}, bf16[64,1,1024]{2,1,...) fusion(bf16[64,16,1024]{2,1,0:T(8,128)(2,1)S(1)} %bitcast.131), kind=kLoop, calls=%fused_computation.127 | loop fusion | bytes 4194304 | tf_op jit(solution)/shard_map/split | solution.py:120
  14.0 0.7 bitcast_dynamic-update-slice_fusion.15
  14.7 0.7 bitcast_dynamic-update-slice_fusion.14
  16.8 0.7 bitcast_dynamic-update-slice_fusion.11
  25.2 7.6 %all-to-all-start = ((bf16[16,64,1,1024]{3,1,2,0:T(8,128)(2,1)}), bf16[16,64,1,1024]{3,1,2,0:T(8,128)(2,1)}, u32[]{:S(2)}, u32[]{:S(2)}) async-start(bf16[16,64,1,1024]{3,1,2,0:T(8,128)(2,1)} %bitcast_dynamic-update-slice_fusion), calls=%async_computation | async-start | bytes 4194304 | tf_op jit(solution)/shard_map/all_to_all | solution.py:118
  32.9 2.2 maximum_maximum_fusion
  35.7 24.3 %all-to-all-done = bf16[16,64,1,1024]{3,1,2,0:T(8,128)(2,1)} async-done(((bf16[16,64,1,1024]{3,1,2,0:T(8,128)(2,1)}), bf16[16,64,1,1024]{3,1,2,0:T(8,128)(2,1)}, u32[]{:S(2)}, u32[]{:S(2)}) %all-to-all-start) | async-done | bytes 2097184 | tf_op jit(solution)/shard_map/all_to_all | solution.py:118
  60.5 0.8 dynamic_slice.11
  61.6 4.0 fusion.8
  65.6 4.9 %fusion = (f32[1024]{0:T(1024)S(1)}, bf16[1024,1024]{1,0:T(8,128)(2,1)S(1)}) fusion(f32[1024,1024]{1,0:T(8,128)S(1)} %fusion.8, bf16[1024,1024]{1,0:T(8,128)(2,1)} %collective-permute-done.3, s32[1024]{0:T(1024)S(1)} %fusion.61, pred[1024]{0:T(1024)(128)(4,1)S(1)} %get-tuple-element.16), kind=kOutput, calls=%fused_computation.10 | convolution fusion | flops 2154822656 | bytes 8397824 | tf_op jit(solution)/shard_map/dot_general | solution.py:153
  70.5 3.6 select_convert_fusion.1
  74.1 44.4 %all_to_all.25 = bf16[16,64,1408]{2,1,0:T(8,128)(2,1)S(1)} all-to-all(bf16[16,64,1408]{2,1,0:T(8,128)(2,1)S(1)} %bitcast.134), channel_id=1, replica_groups=mesh['dp'=16,'section'=2,'tensor'=8] {'dp'}, dimensions={0} | all-to-all | bytes 5767168 | tf_op jit(solution)/shard_map/all_to_all | solution.py:77
  120.2 32.0 %all_to_all.26 = bf16[16,64,1024]{2,1,0:T(8,128)(2,1)S(1)} all-to-all(bf16[16,64,1024]{2,1,0:T(8,128)(2,1)S(1)} %broadcast_in_dim.78), channel_id=1, replica_groups=mesh['dp'=16,'section'=2,'tensor'=8] {'dp'}, dimensions={0} | all-to-all | bytes 4194304 | tf_op jit(solution)/shard_map/all_to_all | solution.py:53
  152.2 5.3 %fusion.30 = bf16[1024,1024]{1,0:T(8,128)(2,1)} fusion(bf16[1024,1024]{1,0:T(8,128)(2,1)S(1)} %bitcast.139, bf16[1024,1024]{1,0:T(8,128)(2,1)} %collective-permute-done.2, pred[]{:T(512)S(6)} %eq.58, bf16[1,1024,1024]{2,1,0:T(8,128)(2,1)} %param.13), kind=kOutput, calls=%fused_computation.39 | convolution fusion | flops 2149580800 | bytes 8388609 | tf_op jit(solution)/shard_map/dot_general | solution.py:91
  157.7 81.9 %all-reduce.3.cloned.1.call-done = bf16[1024,1024]{1,0:T(8,128)(2,1)} async-done(((bf16[1024,1024]{1,0:T(8,128)(2,1)}), bf16[1024,1024]{1,0:T(8,128)(2,1)}) %all-reduce.3.cloned.1.call-update) | async-done | bytes 2097168 | tf_op jit(solution)/shard_map/psum | solution.py:94
  239.6 2.5 fusion.3
  242.5 5.4 %select_convert_fusion = bf16[1024,1408]{1,0:T(8,128)(2,1)S(1)} fusion(bf16[1024,1408]{1,0:T(8,128)(2,1)} %collective-permute-done.1, bf16[1024]{0:T(1024)(128)(2,1)S(1)} %get-tuple-element.36, bf16[1024]{0:T(1024)(128)(2,1)S(1)} %get-tuple-element.35, pred[]{:T(512)S(6)} %eq.59, pred[1408]{0:T(1024)(128)(4,1)S(1)} %get-tuple-element.45, ...), kind=kOutput, calls=%fused_computation.7 | convolution fusion | flops 2973106176 | bytes 12596737 | tf_op jit(solution)/shard_map/dot_general | solution.py:64
  247.9 37.0 %all_to_all.27 = bf16[16,64,1408]{2,1,0:T(8,128)(2,1)S(1)} all-to-all(bf16[16,64,1408]{2,1,0:T(8,128)(2,1)S(1)} %bitcast.133), channel_id=1, replica_groups=mesh['dp'=16,'section'=2,'tensor'=8] {'dp'}, dimensions={0} | all-to-all | bytes 5767168 | tf_op jit(solution)/shard_map/all_to_all | solution.py:77
  286.5 25.5 %all_to_all.28 = bf16[16,64,1024]{2,1,0:T(8,128)(2,1)S(1)} all-to-all(bf16[16,64,1024]{2,1,0:T(8,128)(2,1)S(1)} %broadcast_in_dim.82), channel_id=1, replica_groups=mesh['dp'=16,'section'=2,'tensor'=8] {'dp'}, dimensions={0} | all-to-all | bytes 4194304 | tf_op jit(solution)/shard_map/all_to_all | solution.py:53
  312.0 5.9 %fusion.33 = bf16[1024,1024]{1,0:T(8,128)(2,1)} fusion(bf16[1024,1024]{1,0:T(8,128)(2,1)S(1)} %bitcast.138, bf16[1024,1024]{1,0:T(8,128)(2,1)} %collective-permute-done.2, pred[]{:T(512)S(6)} %eq.59, bf16[1,1024,1024]{2,1,0:T(8,128)(2,1)} %param.13), kind=kOutput, calls=%fused_computation.40 | convolution fusion | flops 2149580800 | bytes 8388609 | tf_op jit(solution)/shard_map/dot_general | solution.py:91
  318.0 77.9 %all-reduce.5.cloned.1.call-done = bf16[1024,1024]{1,0:T(8,128)(2,1)} async-done(((bf16[1024,1024]{1,0:T(8,128)(2,1)}), bf16[1024,1024]{1,0:T(8,128)(2,1)}) %all-reduce.5.cloned.1.call-update) | async-done | bytes 2097168 | tf_op jit(solution)/shard_map/psum | solution.py:94
  395.8 5.0 %fusion.5 = bf16[1024,1024]{1,0:T(8,128)(2,1)} fusion(bf16[1024,1024]{1,0:T(8,128)(2,1)} %all-reduce.5.cloned.1.call-done, bf16[1024,1024]{1,0:T(8,128)(2,1)} %all-reduce.3.cloned.1.call-done, bf16[1024,1024]{1,0:T(8,128)(2,1)S(1)} %get-tuple-element.40), kind=kLoop, calls=%fused_computation.15 | loop fusion | flops 8388608 | bytes 8388608 | tf_op jit(solution)/shard_map/convert_element_type | solution.py:95
  (70 shorter events, 14.4 us)
Async XLA Ops:
  25.2 7.7 %copy-start.3 = (bf16[1,1024,1,256]{3,1,2,0:T(8,128)(2,1)S(1)}, bf16[1,1024,1,256]{3,1,2,0:T(8,128)(2,1)}, u32[]{:S(2)}) copy-start(bf16[1,1024,1,256]{3,1,2,0:T(8,128)(2,1)} %param.12) | copy-start | bytes 1572868
  25.2 34.8 %all-to-all-start = ((bf16[16,64,1,1024]{3,1,2,0:T(8,128)(2,1)}), bf16[16,64,1,1024]{3,1,2,0:T(8,128)(2,1)}, u32[]{:S(2)}, u32[]{:S(2)}) async-start(bf16[16,64,1,1024]{3,1,2,0:T(8,128)(2,1)} %bitcast_dynamic-update-slice_fusion), calls=%async_computation | async-start | bytes 4194304 | tf_op jit(solution)/shard_map/all_to_all | solution.py:118
  32.8 206.8 %all-reduce.3.cloned.1.call-start = ((), (), s32[]{:S(2)}) async-start(), calls=%async_computation.5 | async-start | bytes 4194304 | tf_op jit(solution)/shard_map/psum | solution.py:94
  32.9 27.2 %copy-start.5 = (f32[1,1024]{1,0:T(1,128)S(1)}, f32[1,1024]{1,0:T(1,128)}, u32[]{:S(2)}) copy-start(f32[1,1024]{1,0:T(1,128)} %param.10) | copy-start | bytes 12292
  32.9 28.5 %copy-start.4 = (s32[2048]{0:T(1024)S(1)}, s32[2048]{0:T(1024)}, u32[]{:S(2)}) copy-start(s32[2048]{0:T(1024)} %param.8) | copy-start | bytes 24580
  35.1 30.4 %collective-permute-start.1 = (bf16[1024,1408]{1,0:T(8,128)(2,1)S(1)}, bf16[1024,1408]{1,0:T(8,128)(2,1)}, u32[]{:S(2)}, u32[]{:S(2)}) collective-permute-start(bf16[1024,1408]{1,0:T(8,128)(2,1)S(1)} %maximum_maximum_fusion), channel_id=1, source_target_pairs={{0,8},{8,0},{1,9},{9,1},{2,10},{10,2},{3,11},{11,3},{4,12},{12,4},... | collective-permute-start | bytes 8650760 | tf_op jit(solution)/shard_map/ppermute | solution.py:113
  35.2 30.3 %collective-permute-start.2 = (bf16[1024,1024]{1,0:T(8,128)(2,1)}, bf16[1024,1024]{1,0:T(8,128)(2,1)}, u32[]{:S(2)}, u32[]{:S(2)}) collective-permute-start(bf16[1024,1024]{1,0:T(8,128)(2,1)} %bitcast.4), channel_id=1, source_target_pairs={{0,8},{8,0},{1,9},{9,1},{2,10},{10,2},{3,11},{11,3},{4,12},{12,4},... | collective-permute-start | bytes 6291464 | tf_op jit(solution)/shard_map/ppermute | solution.py:113
  60.0 5.5 %collective-permute-start.3 = (bf16[1024,1024]{1,0:T(8,128)(2,1)}, bf16[1024,1024]{1,0:T(8,128)(2,1)}, u32[]{:S(2)}, u32[]{:S(2)}) collective-permute-start(bf16[1024,1024]{1,0:T(8,128)(2,1)} %bitcast), channel_id=1, source_target_pairs={{0,8},{8,0},{1,9},{9,1},{2,10},{10,2},{3,11},{11,3},{4,12},{12,4},... | collective-permute-start | bytes 6291464 | tf_op jit(solution)/shard_map/ppermute | solution.py:132
  60.0 5.5 %collective-permute-start = (f32[1024]{0:T(1024)S(1)}, f32[1024]{0:T(1024)S(1)}, u32[]{:S(2)}, u32[]{:S(2)}) collective-permute-start(f32[1024]{0:T(1024)S(1)} %bitcast.153), channel_id=1, source_target_pairs={{0,8},{8,0},{1,9},{9,1},{2,10},{10,2},{3,11},{11,3},{4,12},{12,4},... | collective-permute-start | bytes 12296 | tf_op jit(solution)/shard_map/ppermute | solution.py:113
  65.6 4.9 %copy-start.1 = (bf16[1,1024,1024]{2,1,0:T(8,128)(2,1)S(1)}, bf16[1,1024,1024]{2,1,0:T(8,128)(2,1)}, u32[]{:S(2)}) copy-start(bf16[1,1024,1024]{2,1,0:T(8,128)(2,1)} %param.11) | copy-start | bytes 6291460
  157.4 238.4 %all-reduce.5.cloned.1.call-start = ((), (), s32[]{:S(2)}) async-start(), calls=%async_computation.6 | async-start | bytes 4194304 | tf_op jit(solution)/shard_map/psum | solution.py:94
  239.6 2.5 copy-start
  239.6 2.9 copy-start.2
Sparse Core Ops, SparseCore 0:
  157.6 81.9 all-reduce.2
  318.1 77.7 all-reduce.4
